TPU v7x, 256 devices: a whole 4x4x8 slice. The times are simulated.
256 devices in a mesh: blk: 32 (over z, x_lo, core), col: 8 (over x_hi, y).
Axes of the slice: x: 4 (x_hi: 2, x_lo: 2; x = x_hi * 2 + x_lo), y: 4, z: 8, core: 2. Of those that a mesh axis runs over, the one named last changes fastest.
Arguments:
- feat1: bfloat16 [128, 384, 256], P('blk', 'col'), may hold values from -40 to 40
- feat2: bfloat16 [128, 384, 256], P('blk', 'col'), may hold values from -40 to 40
Outputs:
- flow: float32 [2, 128, 384], P(None, 'blk', 'col')
- grad_flow: float32 [2, 128, 384], P(None, 'blk', 'col')
- grad_warped: float32 [128, 384, 256], P('blk', 'col')
All inputs are finite; a program needn't handle non-finite values.
Results may differ from a plain program's by a relative error of at most 0.0075.
Values may be sent and summed in bfloat16 or wider, within the bound.
No kernel may reach another device: no remote copies, remote signals or barrier semaphores. Data moves between devices by JAX's collectives and lax.ppermute only.
A program may use at most 64 MiB of HBM per device.

v0:
```python
import math
import jax
import jax.numpy as jnp
from jax import lax
from jax.sharding import Mesh
from jax.sharding import PartitionSpec as P

ssim_one = 0.01
ssim_two = 0.03
charb_sq = 0.0001
FINE = ("z", "xl", "c", "xh", "y")
BLK = ("z", "xl", "c")
COL = ("xh", "y")
KEY_AXES = ("z", ("xh", "xl"))
QUERY_AXES = ("y", "c")


def with_halo(value, sides, width):
    for axis, dim in sides:
        count, length = (lax.axis_size(axis), value.shape[dim])
        up = [(i, (i + 1) % count) for i in range(count - 1)]
        down = [(j, i) for i, j in up]
        last = lax.slice_in_dim(value, length - width, length, axis=dim)
        first = lax.slice_in_dim(value, 0, width, axis=dim)
        before = lax.ppermute(last, axis, up)
        after = lax.ppermute(first, axis, down)
        value = jnp.concatenate([before, value, after], axis=dim)
    return value


def box_valid(padded):
    rows_out = padded.shape[0] - 2
    cols_out = padded.shape[1] - 2
    total = jnp.zeros((rows_out, cols_out) + padded.shape[2:], padded.dtype)
    for offset_r in range(3):
        for offset_c in range(3):
            total = total + padded[offset_r : offset_r + rows_out, offset_c : offset_c + cols_out]
    return total / 9.0


def ssim_loss(mean_y, var_y, cov_xy, mean_x, var_x):
    top = (2.0 * mean_x * mean_y + ssim_one) * (2.0 * cov_xy + ssim_two)
    bottom = (mean_x * mean_x + mean_y * mean_y + ssim_one) * (var_x + var_y + ssim_two)
    return jnp.sum((1.0 - top / bottom) * 0.5)


def local_terms(xpad, ypad):
    mean_x = box_valid(xpad)
    mean_y = box_valid(ypad)
    var_x = box_valid(xpad * xpad) - mean_x * mean_x
    var_y = box_valid(ypad * ypad) - mean_y * mean_y
    cov_xy = box_valid(xpad * ypad) - mean_x * mean_y
    loss, pull = jax.vjp(
        lambda one, two, three: ssim_loss(one, two, three, mean_x, var_x), mean_y, var_y, cov_xy
    )
    grad_mean, grad_var, grad_cov = pull(jnp.ones_like(loss))
    first = grad_mean - 2.0 * grad_var * mean_y - grad_cov * mean_x
    return (first, grad_var, grad_cov)


def edge_weight(lower, upper):
    return jnp.exp(-jnp.mean(jnp.abs(upper - lower), axis=-1))


def charbonnier(weight, delta):
    return weight * delta / jnp.sqrt(delta * delta + charb_sq)


def absorb(carry, queries, keys, key_y, key_x, scale):
    total_keys = keys.shape[0]
    width = keys.shape[1]
    step = min(total_keys, 2048)
    while total_keys % step != 0:
        step = step - 1
    blocks = total_keys // step

    def visit(state, item):
        top, total, acc, along_y, along_x = state
        key_block, block_y, block_x = item
        score = (
            lax.dot_general(
                queries, key_block, (((1,), (1,)), ((), ())), preferred_element_type=jnp.float32
            )
            * scale
        )
        new_top = jnp.maximum(top, jnp.max(score, axis=1))
        shrink = jnp.exp(top - new_top)
        expo = jnp.exp(score - new_top[:, None])
        total = total * shrink + jnp.sum(expo, axis=1)
        acc = acc * shrink[:, None] + jnp.dot(
            expo.astype(jnp.bfloat16), key_block, preferred_element_type=jnp.float32
        )
        along_y = along_y * shrink + jnp.sum(expo * block_y[None, :], axis=1)
        along_x = along_x * shrink + jnp.sum(expo * block_x[None, :], axis=1)
        return ((new_top, total, acc, along_y, along_x), None)

    items = (
        keys.reshape(blocks, step, width),
        key_y.reshape(blocks, step),
        key_x.reshape(blocks, step),
    )
    carry, unused = lax.scan(visit, carry, items)
    return carry


def body(feat1, feat2):
    rows, cols, width = feat1.shape
    ncol = lax.axis_size(COL)
    full_rows = rows * lax.axis_size(BLK)
    full_cols = cols * ncol
    row_start = lax.axis_index(BLK) * rows
    col_start = lax.axis_index(COL) * cols
    scale = 1.0 / math.sqrt(width)
    tokens = rows * cols
    queries = lax.all_gather(feat1.reshape(tokens, width), QUERY_AXES, axis=0, tiled=True)
    group = queries.shape[0]
    init = (
        jnp.full((group,), -1e30, jnp.float32),
        jnp.zeros((group,), jnp.float32),
        jnp.zeros((group, width), jnp.float32),
        jnp.zeros((group,), jnp.float32),
        jnp.zeros((group,), jnp.float32),
    )

    def norm_y(index):
        return (index.astype(jnp.float32) + 0.5) * (2.0 / full_rows) - 1.0

    def norm_x(index):
        return (index.astype(jnp.float32) + 0.5) * (2.0 / full_cols) - 1.0

    piece = feat2
    for axis in KEY_AXES:
        piece = lax.all_gather(piece, axis, axis=0, tiled=True)
    count = piece.shape[0]
    gathered = jnp.arange(count, dtype=jnp.int32)
    rest = gathered // rows
    place = {}
    for axis in KEY_AXES:
        size = lax.axis_size(axis)
        place[axis] = rest % size
        rest = rest // size
    sz, sxl, sc, sxh, sy = (lax.axis_size(a) for a in FINE)
    x_full = place["xh", "xl"]
    blk_of = (place["z"] * sxl + x_full % sxl) * sc + lax.axis_index("c")
    col_of = x_full // sxl * sy + lax.axis_index("y")
    tile_y = blk_of * rows + gathered % rows
    tile_x = col_of * cols
    grid_y = jnp.broadcast_to(tile_y[:, None], (count, cols))
    grid_x = tile_x[:, None] + jnp.arange(cols, dtype=jnp.int32)[None, :]
    carry = absorb(
        init,
        queries,
        piece.reshape(count * cols, width),
        norm_y(grid_y).reshape(-1),
        norm_x(grid_x).reshape(-1),
        scale,
    )
    top, total, acc, along_y, along_x = carry
    parts = lax.axis_size(QUERY_AXES)
    stats = jnp.stack([top, total, along_y, along_x]).reshape(4, parts, tokens)
    stats = jnp.pad(stats.transpose(1, 0, 2), ((0, 0), (0, 0), (0, width - tokens)))
    packed = jnp.concatenate([acc.reshape(parts, tokens, width), stats], axis=1)
    packed = lax.all_to_all(packed, QUERY_AXES, 0, 0, tiled=True)
    tops = packed[:, tokens, :tokens]
    peak = jnp.max(tops, axis=0)
    factor = jnp.exp(tops - peak[None])
    acc = jnp.sum(packed[:, :tokens, :] * factor[:, :, None], axis=0)
    total = jnp.sum(packed[:, tokens + 1, :tokens] * factor, axis=0)
    along_y = jnp.sum(packed[:, tokens + 2, :tokens] * factor, axis=0)
    along_x = jnp.sum(packed[:, tokens + 3, :tokens] * factor, axis=0)
    warped = (acc / total[:, None]).astype(jnp.bfloat16).reshape(rows, cols, width)
    own_y = norm_y(row_start + jnp.arange(rows, dtype=jnp.int32))
    own_x = norm_x(col_start + jnp.arange(cols, dtype=jnp.int32))
    flow = jnp.stack(
        [
            (along_y / total).reshape(rows, cols) - own_y[:, None],
            (along_x / total).reshape(rows, cols) - own_x[None, :],
        ]
    )
    pair = jnp.stack([feat1, warped])
    xval = feat1.astype(jnp.float32)
    yval = warped.astype(jnp.float32)
    margin = 1
    padded = with_halo(pair, ((BLK, 1), (COL, 2)), 1)
    xpad = padded[0].astype(jnp.float32)
    ypad = padded[1].astype(jnp.float32)
    first, grad_var, grad_cov = local_terms(xpad, ypad)
    maps = jnp.stack([first, grad_var, grad_cov])
    beside_all = with_halo(maps.astype(jnp.bfloat16), ((BLK, 1), (COL, 2)), 1).astype(maps.dtype)
    spread_first = box_valid(beside_all[0])
    spread_var = box_valid(beside_all[1])
    spread_cov = box_valid(beside_all[2])
    grad_warped = spread_first + 2.0 * yval * spread_var + xval * spread_cov
    flow_pad = with_halo(flow, ((BLK, 1), (COL, 2)), 1)
    x_rows = xpad[margin - 1 : margin + rows + 1, margin : margin + cols]
    x_cols = xpad[margin : margin + rows, margin - 1 : margin + cols + 1]
    edge_y = row_start - 1 + jnp.arange(rows + 1, dtype=jnp.int32)
    valid_y = (edge_y >= 0) & (edge_y <= full_rows - 2)
    edge_x = col_start - 1 + jnp.arange(cols + 1, dtype=jnp.int32)
    valid_x = (edge_x >= 0) & (edge_x <= full_cols - 2)
    delta_y = flow_pad[:, 1:, 1:-1] - flow_pad[:, :-1, 1:-1]
    push_y = jnp.where(
        valid_y[None, :, None],
        charbonnier(edge_weight(x_rows[:-1], x_rows[1:])[None], delta_y),
        0.0,
    )
    delta_x = flow_pad[:, 1:-1, 1:] - flow_pad[:, 1:-1, :-1]
    push_x = jnp.where(
        valid_x[None, None, :],
        charbonnier(edge_weight(x_cols[:, :-1], x_cols[:, 1:])[None], delta_x),
        0.0,
    )
    grad_flow = push_y[:, :rows] - push_y[:, 1:] + push_x[:, :, :cols] - push_x[:, :, 1:]
    return (flow, grad_flow, grad_warped)


def solution(mesh):
    blk, col = mesh.devices.shape
    fine = mesh.devices.reshape(blk // 4, 2, 2, 2, col // 2)
    fine_mesh = Mesh(fine, FINE)
    placed = (P(BLK, COL, None), P(BLK, COL, None))
    return jax.shard_map(
        body,
        mesh=fine_mesh,
        in_specs=placed,
        out_specs=(P(None, BLK, COL), P(None, BLK, COL), P(BLK, COL, None)),
        check_vma=False,
    )
```

profile of v0, /device:TPU:132, one launch (start us, length us, event | category | flops | bytes accessed | tf_op | source)
XLA Modules:
  0.0 233.7 jit_solution(6486698609514709676)
XLA Ops:
  7.2 28.3 %all_gather.9 = bf16[32,48,256]{2,1,0:T(8,128)(2,1)} all-gather(bf16[4,48,256]{2,1,0:T(8,128)(2,1)} %param.5), channel_id=1, replica_groups=mesh['z'=8,'xl'=2,'c'=2,'xh'=2,'y'=4] {'z'}, dimensions={0}, use_global_device_ids=true | all-gather | bytes 884736 | tf_op jit(solution)/shard_map/all_gather | solution.py:133
  35.7 0.1 sub.129
  35.8 0.1 multiply_add_fusion.2
  35.9 0.1 reshape.310
  36.0 14.1 %all_gather.11 = bf16[1536,256]{1,0:T(8,128)(2,1)S(1)} all-gather(bf16[192,256]{1,0:T(8,128)(2,1)} %bitcast.82), channel_id=1, replica_groups=mesh['z'=8,'xl'=2,'c'=2,'xh'=2,'y'=4] {'y','c'}, dimensions={0}, use_global_device_ids=true | all-gather | bytes 884736 | tf_op jit(solution)/shard_map/all_gather | solution.py:115
  50.2 27.9 %all-gather.2.cloned.1.call-done = bf16[128,48,256]{2,1,0:T(8,128)(2,1)} async-done(((bf16[32,48,256]{2,1,0:T(8,128)(2,1)}), bf16[128,48,256]{2,1,0:T(8,128)(2,1)}) %all-gather.2.cloned.1.call-update) | async-done | bytes 3145744 | tf_op jit(solution)/shard_map/all_gather | solution.py:133
  78.1 60.4 %while.19 = (s32[]{:T(128)}, f32[1536]{0:T(1024)S(1)}, f32[1536]{0:T(1024)S(1)}, f32[1536,256]{1,0:T(8,128)S(1)}, f32[1536]{0:T(1024)S(1)}, /*index=5*/f32[1536]...) while((s32[]{:T(128)}, f32[1536]{0:T(1024)S(1)}, ...), condition=%wide.region_5.6_spmd.clone, body=%wide.region_0.5_spmd.clone.sunk | while | flops 3260167680 | bytes 94312616 | solution.py:102
  78.1 7.6 %multiply_reduce_fusion.5 = (f32[1536]{0:T(1024)S(1)}, f32[2048,1536]{1,0:T(8,128)}) fusion(bf16[1536,256]{1,0:T(8,128)(2,1)S(1)} %get-tuple-element.282, bf16[3,2048,256]{2,1,0:T(8,128)(2,1)} %get-tuple-element.281, s32[]{:T(128)S(6)} %copy.42), kind=kOutput, calls=%fused_computation.3.clone.1 | convolution fusion | flops 1616902656 | bytes 14424068 | tf_op jit(solution)/shard_map/while/body/eval_jaxpr/dot_general | solution.py:81
  85.7 8.5 %multiply_reduce_fusion.6 = (f32[1536]{0:T(1024)S(1)}, f32[1536]{0:T(1024)S(1)}, f32[1536]{0:T(1024)S(1)}) fusion(f32[2048]{0:T(1024)S(1)} %bitcast.89, f32[1536]{0:T(1024)S(1)} %select_maximum_fusion.3, f32[2048,1536]{1,0:T(8,128)} %get-tuple-element.242, f32[2048]{0:T(1024)S(1)} %bitcast.90), kind=kLoop, calls=%fused_computation.clone.1 | loop fusion | flops 22015488 | bytes 12623872 | tf_op jit(solution)/shard_map/while/body/eval_jaxpr/reduce_sum | solution.py:94
  94.3 3.9 %fusion.89 = f32[1536,256]{1,0:T(8,128)S(1)} fusion(f32[1536]{0:T(1024)S(1)} %select_maximum_fusion.3, f32[2048,1536]{1,0:T(8,128)S(1)} %copy-done, f32[1536,256]{1,0:T(8,128)S(1)} %get-tuple-element.266, bf16[3,2048,256]{2,1,0:T(8,128)(2,1)} %get-tuple-element.281, s32[]{:T(128)S(6)} %copy.42, f32[1536]{0:T(1024)S(1)} %get-tuple-element.246, ...), kind=kOutput, calls=%fused_computation.7.clone.1 | convolution fusion | flops 1621229568 | bytes 16789508 | tf_op jit(solution)/shard_map/while/body/eval_jaxpr/dot_general | solution.py:90
  98.3 7.6 %multiply_reduce_fusion.5 = (f32[1536]{0:T(1024)S(1)}, f32[2048,1536]{1,0:T(8,128)}) fusion(bf16[1536,256]{1,0:T(8,128)(2,1)S(1)} %get-tuple-element.282, bf16[3,2048,256]{2,1,0:T(8,128)(2,1)} %get-tuple-element.281, s32[]{:T(128)S(6)} %copy.42), kind=kOutput, calls=%fused_computation.3.clone.1 | convolution fusion | flops 1616902656 | bytes 14424068 | tf_op jit(solution)/shard_map/while/body/eval_jaxpr/dot_general | solution.py:81
  105.9 8.5 %multiply_reduce_fusion.6 = (f32[1536]{0:T(1024)S(1)}, f32[1536]{0:T(1024)S(1)}, f32[1536]{0:T(1024)S(1)}) fusion(f32[2048]{0:T(1024)S(1)} %bitcast.89, f32[1536]{0:T(1024)S(1)} %select_maximum_fusion.3, f32[2048,1536]{1,0:T(8,128)} %get-tuple-element.242, f32[2048]{0:T(1024)S(1)} %bitcast.90), kind=kLoop, calls=%fused_computation.clone.1 | loop fusion | flops 22015488 | bytes 12623872 | tf_op jit(solution)/shard_map/while/body/eval_jaxpr/reduce_sum | solution.py:94
  114.4 3.9 %fusion.89 = f32[1536,256]{1,0:T(8,128)S(1)} fusion(f32[1536]{0:T(1024)S(1)} %select_maximum_fusion.3, f32[2048,1536]{1,0:T(8,128)S(1)} %copy-done, f32[1536,256]{1,0:T(8,128)S(1)} %get-tuple-element.266, bf16[3,2048,256]{2,1,0:T(8,128)(2,1)} %get-tuple-element.281, s32[]{:T(128)S(6)} %copy.42, f32[1536]{0:T(1024)S(1)} %get-tuple-element.246, ...), kind=kOutput, calls=%fused_computation.7.clone.1 | convolution fusion | flops 1621229568 | bytes 16789508 | tf_op jit(solution)/shard_map/while/body/eval_jaxpr/dot_general | solution.py:90
  118.4 7.6 %multiply_reduce_fusion.5 = (f32[1536]{0:T(1024)S(1)}, f32[2048,1536]{1,0:T(8,128)}) fusion(bf16[1536,256]{1,0:T(8,128)(2,1)S(1)} %get-tuple-element.282, bf16[3,2048,256]{2,1,0:T(8,128)(2,1)} %get-tuple-element.281, s32[]{:T(128)S(6)} %copy.42), kind=kOutput, calls=%fused_computation.3.clone.1 | convolution fusion | flops 1616902656 | bytes 14424068 | tf_op jit(solution)/shard_map/while/body/eval_jaxpr/dot_general | solution.py:81
  126.0 8.5 %multiply_reduce_fusion.6 = (f32[1536]{0:T(1024)S(1)}, f32[1536]{0:T(1024)S(1)}, f32[1536]{0:T(1024)S(1)}) fusion(f32[2048]{0:T(1024)S(1)} %bitcast.89, f32[1536]{0:T(1024)S(1)} %select_maximum_fusion.3, f32[2048,1536]{1,0:T(8,128)} %get-tuple-element.242, f32[2048]{0:T(1024)S(1)} %bitcast.90), kind=kLoop, calls=%fused_computation.clone.1 | loop fusion | flops 22015488 | bytes 12623872 | tf_op jit(solution)/shard_map/while/body/eval_jaxpr/reduce_sum | solution.py:94
  134.6 3.9 %fusion.89 = f32[1536,256]{1,0:T(8,128)S(1)} fusion(f32[1536]{0:T(1024)S(1)} %select_maximum_fusion.3, f32[2048,1536]{1,0:T(8,128)S(1)} %copy-done, f32[1536,256]{1,0:T(8,128)S(1)} %get-tuple-element.266, bf16[3,2048,256]{2,1,0:T(8,128)(2,1)} %get-tuple-element.281, s32[]{:T(128)S(6)} %copy.42, f32[1536]{0:T(1024)S(1)} %get-tuple-element.246, ...), kind=kOutput, calls=%fused_computation.7.clone.1 | convolution fusion | flops 1621229568 | bytes 16789508 | tf_op jit(solution)/shard_map/while/body/eval_jaxpr/dot_general | solution.py:90
  138.9 1.3 select_maximum_fusion.1
  140.2 4.4 %all-to-all-start = ((f32[8,196,256]{2,1,0:T(8,128)}), f32[8,196,256]{2,1,0:T(8,128)S(1)}, u32[]{:S(2)}, u32[]{:S(2)}) async-start(f32[8,196,256]{2,1,0:T(8,128)} %select_maximum_fusion.1), calls=%async_computation | async-start | bytes 3276800 | tf_op jit(solution)/shard_map/all_to_all | solution.py:163
  144.7 22.2 %all-to-all-done = f32[8,196,256]{2,1,0:T(8,128)S(1)} async-done(((f32[8,196,256]{2,1,0:T(8,128)}), f32[8,196,256]{2,1,0:T(8,128)S(1)}, u32[]{:S(2)}, u32[]{:S(2)}) %all-to-all-start) | async-done | bytes 1605664 | tf_op jit(solution)/shard_map/all_to_all | solution.py:163
  167.1 0.1 div.141
  167.3 1.9 collective-permute-start.4
  169.3 2.4 %collective-permute-start.5 = (f32[2,1,48]{2,1,0:T(1,128)S(1)}, f32[2,1,48]{2,1,0:T(1,128)S(1)}, u32[]{:S(2)}, u32[]{:S(2)}) collective-permute-start(f32[2,1,48]{2,1,0:T(1,128)S(1)} %get-tuple-element.162), channel_id=1, source_target_pairs={{0,8},{8,16},{16,24},{24,32},{32,40},{40,48},{48,56},{56,64},{64,7... | collective-permute-start | bytes 1160 | tf_op jit(solution)/shard_map/ppermute | solution.py:25
  171.7 0.3 fusion.17
  171.9 0.1 divide_convert_fusion.1
  172.1 0.6 pad_maximum_fusion.16
  172.7 5.3 %collective-permute-start.1 = (bf16[2,1,48,256]{3,2,1,0:T(8,128)(2,1)S(1)}, bf16[2,1,48,256]{3,2,1,0:T(8,128)(2,1)S(1)}, u32[]{:S(2)}, u32[]{:S(2)}) collective-permute-start(bf16[2,1,48,256]{3,2,1,0:T(8,128)(2,1)S(1)} %get-tuple-element.159), channel_id=1, source_target_pairs={{8,0},{16,8},{24,16},{32,24},{40,32},{48,40},{56,48},{64,56},{72,6... | collective-permute-start | bytes 147464 | tf_op jit(solution)/shard_map/ppermute | solution.py:26
  177.9 1.9 collective-permute-start
  179.9 5.5 %collective-permute-done = bf16[2,1,48,256]{3,2,1,0:T(8,128)(2,1)S(1)} collective-permute-done((bf16[2,1,48,256]{3,2,1,0:T(8,128)(2,1)S(1)}, bf16[2,1,48,256]{3,2,1,0:T(8,128)(2,1)S(1)}, u32[]{:S(2)}, u32[]{:S(2)}) %collective-permute-start) | collective-permute-done | bytes 49184 | tf_op jit(solution)/shard_map/ppermute | solution.py:25
  185.5 4.1 %collective-permute-start.3 = (bf16[2,6,1,256]{3,2,1,0:T(2,128)(2,1)S(1)}, bf16[2,6,1,256]{3,2,1,0:T(2,128)(2,1)S(1)}, u32[]{:S(2)}, u32[]{:S(2)}) collective-permute-start(bf16[2,6,1,256]{3,2,1,0:T(2,128)(2,1)S(1)} %get-tuple-element.157), channel_id=1, source_target_pairs={{1,0},{2,1},{3,2},{4,3},{5,4},{6,5},{7,6},{9,8},{10,9},{11,10},{12... | collective-permute-start | bytes 18440 | tf_op jit(solution)/shard_map/ppermute | solution.py:26
  189.6 1.9 collective-permute-start.2
  191.6 2.3 collective-permute-start.7
  193.9 7.2 %collective-permute-start.6 = (f32[2,6,1]{2,1,0:T(8,128)S(1)}, f32[2,6,1]{2,1,0:T(8,128)S(1)}, u32[]{:S(2)}, u32[]{:S(2)}) collective-permute-start(f32[2,6,1]{2,1,0:T(8,128)S(1)} %get-tuple-element.160), channel_id=1, source_target_pairs={{1,0},{2,1},{3,2},{4,3},{5,4},{6,5},{7,6},{9,8},{10,9},{11,10},{12... | collective-permute-start | bytes 152 | tf_op jit(solution)/shard_map/ppermute | solution.py:26
  201.1 0.1 pad_maximum_fusion
  201.3 0.1 fusion.21
  201.4 0.1 fusion.19
  201.5 0.1 fusion.47
  201.7 0.8 fusion.51
  202.4 0.1 convert_bitcast_fusion
  202.6 1.9 collective-permute-start.9
  204.5 2.4 %collective-permute-start.8 = (bf16[3,1,48,256]{3,2,1,0:T(8,128)(2,1)S(1)}, bf16[3,1,48,256]{3,2,1,0:T(8,128)(2,1)S(1)}, u32[]{:S(2)}, u32[]{:S(2)}) collective-permute-start(bf16[3,1,48,256]{3,2,1,0:T(8,128)(2,1)S(1)} %get-tuple-element.154), channel_id=1, source_target_pairs={{0,8},{8,16},{16,24},{24,32},{32,40},{40,48},{48,56},{56,64},{64,7... | collective-permute-start | bytes 221192 | tf_op jit(solution)/shard_map/ppermute | solution.py:25
  207.0 0.1 multiply_select_fusion.1
  207.1 5.2 %collective-permute-done.8 = bf16[3,1,48,256]{3,2,1,0:T(8,128)(2,1)S(1)} collective-permute-done((bf16[3,1,48,256]{3,2,1,0:T(8,128)(2,1)S(1)}, bf16[3,1,48,256]{3,2,1,0:T(8,128)(2,1)S(1)}, u32[]{:S(2)}, u32[]{:S(2)}) %collective-permute-start.8) | collective-permute-done | bytes 73760 | tf_op jit(solution)/shard_map/ppermute | solution.py:25
  212.4 3.9 %collective-permute-start.11 = (bf16[3,6,1,256]{3,2,1,0:T(2,128)(2,1)S(1)}, bf16[3,6,1,256]{3,2,1,0:T(2,128)(2,1)S(1)}, u32[]{:S(2)}, u32[]{:S(2)}) collective-permute-start(bf16[3,6,1,256]{3,2,1,0:T(2,128)(2,1)S(1)} %get-tuple-element.148), channel_id=1, source_target_pairs={{1,0},{2,1},{3,2},{4,3},{5,4},{6,5},{7,6},{9,8},{10,9},{11,10},{12... | collective-permute-start | bytes 27656 | tf_op jit(solution)/shard_map/ppermute | solution.py:26
  216.3 1.9 collective-permute-start.10
  218.2 0.7 slice_subtract_fusion.2
  218.9 6.7 %collective-permute-done.10 = bf16[3,6,1,256]{3,2,1,0:T(2,128)(2,1)S(1)} collective-permute-done((bf16[3,6,1,256]{3,2,1,0:T(2,128)(2,1)S(1)}, bf16[3,6,1,256]{3,2,1,0:T(2,128)(2,1)S(1)}, u32[]{:S(2)}, u32[]{:S(2)}) %collective-permute-start.10) | collective-permute-done | bytes 9248 | tf_op jit(solution)/shard_map/ppermute | solution.py:25
  225.6 0.1 maximum_convert_fusion
  225.8 1.0 fusion.24
  (69 shorter events, 1.5 us)
Async XLA Ops:
  7.2 70.9 %all-gather.2.cloned.1.call-start = ((), (), s32[]{:S(2)}) async-start(), calls=%async_computation.1 | async-start | bytes 3932160 | tf_op jit(solution)/shard_map/all_gather | solution.py:133
  85.7 8.5 %copy-start = (f32[2048,1536]{1,0:T(8,128)S(1)}, f32[2048,1536]{1,0:T(8,128)}, u32[]{:S(2)}) copy-start(f32[2048,1536]{1,0:T(8,128)} %get-tuple-element.242) | copy-start | bytes 37748740 | tf_op jit(solution)/shard_map/while
  105.9 8.5 %copy-start = (f32[2048,1536]{1,0:T(8,128)S(1)}, f32[2048,1536]{1,0:T(8,128)}, u32[]{:S(2)}) copy-start(f32[2048,1536]{1,0:T(8,128)} %get-tuple-element.242) | copy-start | bytes 37748740 | tf_op jit(solution)/shard_map/while
  126.0 8.5 %copy-start = (f32[2048,1536]{1,0:T(8,128)S(1)}, f32[2048,1536]{1,0:T(8,128)}, u32[]{:S(2)}) copy-start(f32[2048,1536]{1,0:T(8,128)} %get-tuple-element.242) | copy-start | bytes 37748740 | tf_op jit(solution)/shard_map/while
  140.2 31.8 %copy-start.1 = (bf16[4,48,256]{2,1,0:T(8,128)(2,1)S(1)}, bf16[4,48,256]{2,1,0:T(8,128)(2,1)}, u32[]{:S(2)}) copy-start(bf16[4,48,256]{2,1,0:T(8,128)(2,1)} %param.4) | copy-start | bytes 294916
  140.2 26.7 %all-to-all-start = ((f32[8,196,256]{2,1,0:T(8,128)}), f32[8,196,256]{2,1,0:T(8,128)S(1)}, u32[]{:S(2)}, u32[]{:S(2)}) async-start(f32[8,196,256]{2,1,0:T(8,128)} %select_maximum_fusion.1), calls=%async_computation | async-start | bytes 3276800 | tf_op jit(solution)/shard_map/all_to_all | solution.py:163
  167.3 12.5 %collective-permute-start.4 = (f32[2,1,48]{2,1,0:T(1,128)S(1)}, f32[2,1,48]{2,1,0:T(1,128)S(1)}, u32[]{:S(2)}, u32[]{:S(2)}) collective-permute-start(f32[2,1,48]{2,1,0:T(1,128)S(1)} %get-tuple-element.163), channel_id=1, source_target_pairs={{8,0},{16,8},{24,16},{32,24},{40,32},{48,40},{56,48},{64,56},{72,6... | collective-permute-start | bytes 1160 | tf_op jit(solution)/shard_map/ppermute | solution.py:26
  169.3 10.6 %collective-permute-start.5 = (f32[2,1,48]{2,1,0:T(1,128)S(1)}, f32[2,1,48]{2,1,0:T(1,128)S(1)}, u32[]{:S(2)}, u32[]{:S(2)}) collective-permute-start(f32[2,1,48]{2,1,0:T(1,128)S(1)} %get-tuple-element.162), channel_id=1, source_target_pairs={{0,8},{8,16},{16,24},{24,32},{32,40},{40,48},{48,56},{56,64},{64,7... | collective-permute-start | bytes 1160 | tf_op jit(solution)/shard_map/ppermute | solution.py:25
  172.7 7.2 %collective-permute-start.1 = (bf16[2,1,48,256]{3,2,1,0:T(8,128)(2,1)S(1)}, bf16[2,1,48,256]{3,2,1,0:T(8,128)(2,1)S(1)}, u32[]{:S(2)}, u32[]{:S(2)}) collective-permute-start(bf16[2,1,48,256]{3,2,1,0:T(8,128)(2,1)S(1)} %get-tuple-element.159), channel_id=1, source_target_pairs={{8,0},{16,8},{24,16},{32,24},{40,32},{48,40},{56,48},{64,56},{72,6... | collective-permute-start | bytes 147464 | tf_op jit(solution)/shard_map/ppermute | solution.py:26
  177.9 7.5 %collective-permute-start = (bf16[2,1,48,256]{3,2,1,0:T(8,128)(2,1)S(1)}, bf16[2,1,48,256]{3,2,1,0:T(8,128)(2,1)S(1)}, u32[]{:S(2)}, u32[]{:S(2)}) collective-permute-start(bf16[2,1,48,256]{3,2,1,0:T(8,128)(2,1)S(1)} %get-tuple-element.158), channel_id=1, source_target_pairs={{0,8},{8,16},{16,24},{24,32},{32,40},{40,48},{48,56},{56,64},{64,7... | collective-permute-start | bytes 147464 | tf_op jit(solution)/shard_map/ppermute | solution.py:25
  185.5 15.6 %collective-permute-start.3 = (bf16[2,6,1,256]{3,2,1,0:T(2,128)(2,1)S(1)}, bf16[2,6,1,256]{3,2,1,0:T(2,128)(2,1)S(1)}, u32[]{:S(2)}, u32[]{:S(2)}) collective-permute-start(bf16[2,6,1,256]{3,2,1,0:T(2,128)(2,1)S(1)} %get-tuple-element.157), channel_id=1, source_target_pairs={{1,0},{2,1},{3,2},{4,3},{5,4},{6,5},{7,6},{9,8},{10,9},{11,10},{12... | collective-permute-start | bytes 18440 | tf_op jit(solution)/shard_map/ppermute | solution.py:26
  189.6 11.5 %collective-permute-start.2 = (bf16[2,6,1,256]{3,2,1,0:T(2,128)(2,1)S(1)}, bf16[2,6,1,256]{3,2,1,0:T(2,128)(2,1)S(1)}, u32[]{:S(2)}, u32[]{:S(2)}) collective-permute-start(bf16[2,6,1,256]{3,2,1,0:T(2,128)(2,1)S(1)} %get-tuple-element.156), channel_id=1, source_target_pairs={{0,1},{1,2},{2,3},{3,4},{4,5},{5,6},{6,7},{8,9},{9,10},{10,11},{11... | collective-permute-start | bytes 18440 | tf_op jit(solution)/shard_map/ppermute | solution.py:25
  191.6 15.4 %collective-permute-start.7 = (f32[2,6,1]{2,1,0:T(8,128)S(1)}, f32[2,6,1]{2,1,0:T(8,128)S(1)}, u32[]{:S(2)}, u32[]{:S(2)}) collective-permute-start(f32[2,6,1]{2,1,0:T(8,128)S(1)} %get-tuple-element.161), channel_id=1, source_target_pairs={{0,1},{1,2},{2,3},{3,4},{4,5},{5,6},{6,7},{8,9},{9,10},{10,11},{11... | collective-permute-start | bytes 152 | tf_op jit(solution)/shard_map/ppermute | solution.py:25
  193.9 13.1 %collective-permute-start.6 = (f32[2,6,1]{2,1,0:T(8,128)S(1)}, f32[2,6,1]{2,1,0:T(8,128)S(1)}, u32[]{:S(2)}, u32[]{:S(2)}) collective-permute-start(f32[2,6,1]{2,1,0:T(8,128)S(1)} %get-tuple-element.160), channel_id=1, source_target_pairs={{1,0},{2,1},{3,2},{4,3},{5,4},{6,5},{7,6},{9,8},{10,9},{11,10},{12... | collective-permute-start | bytes 152 | tf_op jit(solution)/shard_map/ppermute | solution.py:26
  202.6 4.5 %collective-permute-start.9 = (bf16[3,1,48,256]{3,2,1,0:T(8,128)(2,1)S(1)}, bf16[3,1,48,256]{3,2,1,0:T(8,128)(2,1)S(1)}, u32[]{:S(2)}, u32[]{:S(2)}) collective-permute-start(bf16[3,1,48,256]{3,2,1,0:T(8,128)(2,1)S(1)} %get-tuple-element.155), channel_id=1, source_target_pairs={{8,0},{16,8},{24,16},{32,24},{40,32},{48,40},{56,48},{64,56},{72,6... | collective-permute-start | bytes 221192 | tf_op jit(solution)/shard_map/ppermute | solution.py:26
  204.5 7.8 %collective-permute-start.8 = (bf16[3,1,48,256]{3,2,1,0:T(8,128)(2,1)S(1)}, bf16[3,1,48,256]{3,2,1,0:T(8,128)(2,1)S(1)}, u32[]{:S(2)}, u32[]{:S(2)}) collective-permute-start(bf16[3,1,48,256]{3,2,1,0:T(8,128)(2,1)S(1)} %get-tuple-element.154), channel_id=1, source_target_pairs={{0,8},{8,16},{16,24},{24,32},{32,40},{40,48},{48,56},{56,64},{64,7... | collective-permute-start | bytes 221192 | tf_op jit(solution)/shard_map/ppermute | solution.py:25
  212.4 6.5 %collective-permute-start.11 = (bf16[3,6,1,256]{3,2,1,0:T(2,128)(2,1)S(1)}, bf16[3,6,1,256]{3,2,1,0:T(2,128)(2,1)S(1)}, u32[]{:S(2)}, u32[]{:S(2)}) collective-permute-start(bf16[3,6,1,256]{3,2,1,0:T(2,128)(2,1)S(1)} %get-tuple-element.148), channel_id=1, source_target_pairs={{1,0},{2,1},{3,2},{4,3},{5,4},{6,5},{7,6},{9,8},{10,9},{11,10},{12... | collective-permute-start | bytes 27656 | tf_op jit(solution)/shard_map/ppermute | solution.py:26
  216.3 9.3 %collective-permute-start.10 = (bf16[3,6,1,256]{3,2,1,0:T(2,128)(2,1)S(1)}, bf16[3,6,1,256]{3,2,1,0:T(2,128)(2,1)S(1)}, u32[]{:S(2)}, u32[]{:S(2)}) collective-permute-start(bf16[3,6,1,256]{3,2,1,0:T(2,128)(2,1)S(1)} %get-tuple-element.147), channel_id=1, source_target_pairs={{0,1},{1,2},{2,3},{3,4},{4,5},{5,6},{6,7},{8,9},{9,10},{10,11},{11... | collective-permute-start | bytes 27656 | tf_op jit(solution)/shard_map/ppermute | solution.py:25
Sparse Core Ops, SparseCore 0:
  35.6 42.4 all-gather.1
where the time goes:
time: 234 us
  waiting for transfers between devices  67.6 us (29%)
  blocking collectives  42.4 us (18%)
  starting transfers between devices  41.6 us (18%)
  matrix products  34.6 us (15%)
  other arithmetic  31.7 us (14%)
  between operations  14.4 us (6%)
    all_gather x1, blocking collectives, body(): piece = lax.all_gather(piece, axis, axis=0, tiled=True)  28.3 us
    all_gather x1, waiting for transfers between devices, body(): piece = lax.all_gather(piece, axis, axis=0, tiled=True)  27.9 us
    reduce_sum x3, other arithmetic, visit(): along_x = along_x * shrink + jnp.sum(expo * block_x[None, :], axis=1)  25.5 us
    ppermute x6, starting transfers between devices, with_halo(): after = lax.ppermute(first, axis, down)  24.3 us
    dot_general x3, matrix products, visit(): lax.dot_general(queries, key_block, (((1,), (1,)), ((), ())), preferred_e...  22.8 us
    all_to_all x1, waiting for transfers between devices, body(): packed = lax.all_to_all(packed, QUERY_AXES, 0, 0, tiled=True)  22.2 us
    ppermute x6, waiting for transfers between devices, with_halo(): before = lax.ppermute(last, axis, up)  17.4 us
    all_gather x1, blocking collectives, body(): lax.all_gather(feat1.reshape(tokens, width), QUERY_AXES, axis=0, tiled=True)  14.1 us
  transfers between devices with their start and end apart: 14, of which 5 were waited for; matrix products, arithmetic and copies ran while one was open for 2% of the time, Pallas kernels for 0%

commit v1 on v0

--- a/solution.py
+++ b/solution.py
@@ -112,7 +112,10 @@
     col_start = lax.axis_index(COL) * cols
     scale = 1.0 / math.sqrt(width)
     tokens = rows * cols
-    queries = lax.all_gather(feat1.reshape(tokens, width), QUERY_AXES, axis=0, tiled=True)
+    piece_in = feat1.reshape(tokens, width)
+    all_values = jnp.stack([piece_in for _ in range(lax.axis_size(QUERY_AXES))])
+    taken_in = lax.all_to_all(all_values, axis_name=QUERY_AXES, split_axis=0, concat_axis=0)
+    queries = jnp.concatenate(taken_in, 0)
     group = queries.shape[0]
     init = (
         jnp.full((group,), -1e30, jnp.float32),

time: 234 us -> 234 us (level)
  blocking collectives: 42.4 us -> 28.3 us
  waiting for transfers between devices: 67.6 us -> 75.4 us
  starting transfers between devices: 41.6 us -> 46.1 us
    all_gather x1 -> x0, blocking collectives: 14.1 us -> none  [body(): lax.all_gather(feat1.reshape(tokens, width), QUERY_AXES, axis=0, tiled=True)]
    all_to_all x0 -> x1, waiting for transfers between devices: none -> 12.6 us  [body(): lax.all_to_all(all_values, axis_name=QUERY_AXES, split_axis=0, concat_axi...]
    all_gather x1, waiting for transfers between devices: 27.9 us -> 23.1 us  [body(): piece = lax.all_gather(piece, axis, axis=0, tiled=True)]
    all_to_all x0 -> x1, starting transfers between devices: none -> 4.47 us  [body(): lax.all_to_all(all_values, axis_name=QUERY_AXES, split_axis=0, concat_axi...]
  transfers between devices with their start and end apart: 14 -> 15, of which waited for: 5 -> 6; matrix products, arithmetic and copies ran while one was open for 2% -> 2% of each run, Pallas kernels for 0% -> 0%
where the time goes in v1:
time: 234 us; the launch traced here: 233 us
  waiting for transfers between devices  75.4 us (32%)
  starting transfers between devices  46.1 us (20%)
  matrix products  34.6 us (15%)
  other arithmetic  31.6 us (14%)
  blocking collectives  28.3 us (12%)
  between operations  14.4 us (6%)
  local copies, waits for them, and re-layouts  2.94 us (1%)
    all_gather x1, blocking collectives, body(): piece = lax.all_gather(piece, axis, axis=0, tiled=True)  28.3 us
    reduce_sum x3, other arithmetic, visit(): along_x = along_x * shrink + jnp.sum(expo * block_x[None, :], axis=1)  25.3 us
    ppermute x6, starting transfers between devices, with_halo(): after = lax.ppermute(first, axis, down)  24.3 us
    all_gather x1, waiting for transfers between devices, body(): piece = lax.all_gather(piece, axis, axis=0, tiled=True)  23.1 us
    dot_general x3, matrix products, visit(): lax.dot_general(queries, key_block, (((1,), (1,)), ((), ())), preferred_e...  22.8 us
    all_to_all x1, waiting for transfers between devices, body(): packed = lax.all_to_all(packed, QUERY_AXES, 0, 0, tiled=True)  22.2 us
    ppermute x6, waiting for transfers between devices, with_halo(): before = lax.ppermute(last, axis, up)  17.4 us
    ppermute x6, starting transfers between devices, with_halo(): before = lax.ppermute(last, axis, up)  12.8 us
  transfers between devices with their start and end apart: 15, of which 6 were waited for; matrix products, arithmetic and copies ran while one was open for 2% of the time, Pallas kernels for 0%

profile of v1, /device:TPU:132, one launch (start us, length us, event | category | flops | bytes accessed | tf_op | source)
XLA Modules:
  0.0 233.5 jit_solution(8043925656016477180)
XLA Ops:
  7.2 28.3 %all_gather.6 = bf16[32,48,256]{2,1,0:T(8,128)(2,1)} all-gather(bf16[4,48,256]{2,1,0:T(8,128)(2,1)} %param.5), channel_id=1, replica_groups=mesh['z'=8,'xl'=2,'c'=2,'xh'=2,'y'=4] {'z'}, dimensions={0}, use_global_device_ids=true | all-gather | bytes 884736 | tf_op jit(solution)/shard_map/all_gather | solution.py:136
  35.5 1.9 stack.45
  37.4 4.5 %all-to-all-start = ((bf16[8,192,256]{2,1,0:T(8,128)(2,1)}), bf16[8,192,256]{2,1,0:T(8,128)(2,1)S(1)}, u32[]{:S(2)}, u32[]{:S(2)}) async-start(bf16[8,192,256]{2,1,0:T(8,128)(2,1)} %stack.45), calls=%async_computation | async-start | bytes 1572864 | tf_op jit(solution)/shard_map/all_to_all | solution.py:117
  42.0 0.1 sub.129
  42.1 0.1 multiply_add_fusion.2
  42.2 0.1 reshape.312
  42.3 12.6 %all-to-all-done = bf16[8,192,256]{2,1,0:T(8,128)(2,1)S(1)} async-done(((bf16[8,192,256]{2,1,0:T(8,128)(2,1)}), bf16[8,192,256]{2,1,0:T(8,128)(2,1)S(1)}, u32[]{:S(2)}, u32[]{:S(2)}) %all-to-all-start) | async-done | bytes 786464 | tf_op jit(solution)/shard_map/all_to_all | solution.py:117
  55.0 23.1 %all-gather.2.cloned.1.call-done = bf16[128,48,256]{2,1,0:T(8,128)(2,1)} async-done(((bf16[32,48,256]{2,1,0:T(8,128)(2,1)}), bf16[128,48,256]{2,1,0:T(8,128)(2,1)}) %all-gather.2.cloned.1.call-update) | async-done | bytes 3145744 | tf_op jit(solution)/shard_map/all_gather | solution.py:136
  78.1 60.3 %while.19 = (s32[]{:T(128)}, f32[1536]{0:T(1024)S(1)}, f32[1536]{0:T(1024)S(1)}, f32[1536,256]{1,0:T(8,128)S(1)}, f32[1536]{0:T(1024)S(1)}, /*index=5*/f32[1536]...) while((s32[]{:T(128)}, f32[1536]{0:T(1024)S(1)}, ...), condition=%wide.region_5.6_spmd.clone, body=%wide.region_0.5_spmd.clone.sunk | while | flops 3260167680 | bytes 94312616 | solution.py:102
  78.1 7.6 %multiply_reduce_fusion.5 = (f32[1536]{0:T(1024)S(1)}, f32[2048,1536]{1,0:T(8,128)}) fusion(bf16[1536,256]{1,0:T(8,128)(2,1)S(1)} %get-tuple-element.282, bf16[3,2048,256]{2,1,0:T(8,128)(2,1)} %get-tuple-element.281, s32[]{:T(128)S(6)} %copy.42), kind=kOutput, calls=%fused_computation.3.clone.1 | convolution fusion | flops 1616902656 | bytes 14424068 | tf_op jit(solution)/shard_map/while/body/eval_jaxpr/dot_general | solution.py:81
  85.7 8.4 %multiply_reduce_fusion.6 = (f32[1536]{0:T(1024)S(1)}, f32[1536]{0:T(1024)S(1)}, f32[1536]{0:T(1024)S(1)}) fusion(f32[2048]{0:T(1024)S(1)} %bitcast.91, f32[1536]{0:T(1024)S(1)} %select_maximum_fusion.3, f32[2048,1536]{1,0:T(8,128)} %get-tuple-element.242, f32[2048]{0:T(1024)S(1)} %bitcast.92), kind=kLoop, calls=%fused_computation.clone.1 | loop fusion | flops 22015488 | bytes 12623872 | tf_op jit(solution)/shard_map/while/body/eval_jaxpr/reduce_sum | solution.py:94
  94.2 3.9 %fusion.89 = f32[1536,256]{1,0:T(8,128)S(1)} fusion(f32[1536]{0:T(1024)S(1)} %select_maximum_fusion.3, f32[2048,1536]{1,0:T(8,128)S(1)} %copy-done, f32[1536,256]{1,0:T(8,128)S(1)} %get-tuple-element.266, bf16[3,2048,256]{2,1,0:T(8,128)(2,1)} %get-tuple-element.281, s32[]{:T(128)S(6)} %copy.42, f32[1536]{0:T(1024)S(1)} %get-tuple-element.246, ...), kind=kOutput, calls=%fused_computation.7.clone.1 | convolution fusion | flops 1621229568 | bytes 16789508 | tf_op jit(solution)/shard_map/while/body/eval_jaxpr/dot_general | solution.py:90
  98.2 7.6 %multiply_reduce_fusion.5 = (f32[1536]{0:T(1024)S(1)}, f32[2048,1536]{1,0:T(8,128)}) fusion(bf16[1536,256]{1,0:T(8,128)(2,1)S(1)} %get-tuple-element.282, bf16[3,2048,256]{2,1,0:T(8,128)(2,1)} %get-tuple-element.281, s32[]{:T(128)S(6)} %copy.42), kind=kOutput, calls=%fused_computation.3.clone.1 | convolution fusion | flops 1616902656 | bytes 14424068 | tf_op jit(solution)/shard_map/while/body/eval_jaxpr/dot_general | solution.py:81
  105.8 8.4 %multiply_reduce_fusion.6 = (f32[1536]{0:T(1024)S(1)}, f32[1536]{0:T(1024)S(1)}, f32[1536]{0:T(1024)S(1)}) fusion(f32[2048]{0:T(1024)S(1)} %bitcast.91, f32[1536]{0:T(1024)S(1)} %select_maximum_fusion.3, f32[2048,1536]{1,0:T(8,128)} %get-tuple-element.242, f32[2048]{0:T(1024)S(1)} %bitcast.92), kind=kLoop, calls=%fused_computation.clone.1 | loop fusion | flops 22015488 | bytes 12623872 | tf_op jit(solution)/shard_map/while/body/eval_jaxpr/reduce_sum | solution.py:94
  114.3 3.9 %fusion.89 = f32[1536,256]{1,0:T(8,128)S(1)} fusion(f32[1536]{0:T(1024)S(1)} %select_maximum_fusion.3, f32[2048,1536]{1,0:T(8,128)S(1)} %copy-done, f32[1536,256]{1,0:T(8,128)S(1)} %get-tuple-element.266, bf16[3,2048,256]{2,1,0:T(8,128)(2,1)} %get-tuple-element.281, s32[]{:T(128)S(6)} %copy.42, f32[1536]{0:T(1024)S(1)} %get-tuple-element.246, ...), kind=kOutput, calls=%fused_computation.7.clone.1 | convolution fusion | flops 1621229568 | bytes 16789508 | tf_op jit(solution)/shard_map/while/body/eval_jaxpr/dot_general | solution.py:90
  118.3 7.6 %multiply_reduce_fusion.5 = (f32[1536]{0:T(1024)S(1)}, f32[2048,1536]{1,0:T(8,128)}) fusion(bf16[1536,256]{1,0:T(8,128)(2,1)S(1)} %get-tuple-element.282, bf16[3,2048,256]{2,1,0:T(8,128)(2,1)} %get-tuple-element.281, s32[]{:T(128)S(6)} %copy.42), kind=kOutput, calls=%fused_computation.3.clone.1 | convolution fusion | flops 1616902656 | bytes 14424068 | tf_op jit(solution)/shard_map/while/body/eval_jaxpr/dot_general | solution.py:81
  125.9 8.4 %multiply_reduce_fusion.6 = (f32[1536]{0:T(1024)S(1)}, f32[1536]{0:T(1024)S(1)}, f32[1536]{0:T(1024)S(1)}) fusion(f32[2048]{0:T(1024)S(1)} %bitcast.91, f32[1536]{0:T(1024)S(1)} %select_maximum_fusion.3, f32[2048,1536]{1,0:T(8,128)} %get-tuple-element.242, f32[2048]{0:T(1024)S(1)} %bitcast.92), kind=kLoop, calls=%fused_computation.clone.1 | loop fusion | flops 22015488 | bytes 12623872 | tf_op jit(solution)/shard_map/while/body/eval_jaxpr/reduce_sum | solution.py:94
  134.4 3.9 %fusion.89 = f32[1536,256]{1,0:T(8,128)S(1)} fusion(f32[1536]{0:T(1024)S(1)} %select_maximum_fusion.3, f32[2048,1536]{1,0:T(8,128)S(1)} %copy-done, f32[1536,256]{1,0:T(8,128)S(1)} %get-tuple-element.266, bf16[3,2048,256]{2,1,0:T(8,128)(2,1)} %get-tuple-element.281, s32[]{:T(128)S(6)} %copy.42, f32[1536]{0:T(1024)S(1)} %get-tuple-element.246, ...), kind=kOutput, calls=%fused_computation.7.clone.1 | convolution fusion | flops 1621229568 | bytes 16789508 | tf_op jit(solution)/shard_map/while/body/eval_jaxpr/dot_general | solution.py:90
  138.7 1.3 select_maximum_fusion.1
  140.1 4.4 %all-to-all-start.1 = ((f32[8,196,256]{2,1,0:T(8,128)}), f32[8,196,256]{2,1,0:T(8,128)S(1)}, u32[]{:S(2)}, u32[]{:S(2)}) async-start(f32[8,196,256]{2,1,0:T(8,128)} %select_maximum_fusion.1), calls=%async_computation.1 | async-start | bytes 3276800 | tf_op jit(solution)/shard_map/all_to_all | solution.py:166
  144.6 22.2 %all-to-all-done.1 = f32[8,196,256]{2,1,0:T(8,128)S(1)} async-done(((f32[8,196,256]{2,1,0:T(8,128)}), f32[8,196,256]{2,1,0:T(8,128)S(1)}, u32[]{:S(2)}, u32[]{:S(2)}) %all-to-all-start.1) | async-done | bytes 1605664 | tf_op jit(solution)/shard_map/all_to_all | solution.py:166
  167.2 1.9 collective-permute-start.4
  169.1 2.4 %collective-permute-start.5 = (f32[2,1,48]{2,1,0:T(1,128)S(1)}, f32[2,1,48]{2,1,0:T(1,128)S(1)}, u32[]{:S(2)}, u32[]{:S(2)}) collective-permute-start(f32[2,1,48]{2,1,0:T(1,128)S(1)} %get-tuple-element.162), channel_id=1, source_target_pairs={{0,8},{8,16},{16,24},{24,32},{32,40},{40,48},{48,56},{56,64},{64,7... | collective-permute-start | bytes 1160 | tf_op jit(solution)/shard_map/ppermute | solution.py:25
  171.5 0.3 fusion.17
  171.8 0.1 divide_convert_fusion.1
  171.9 0.6 pad_maximum_fusion.16
  172.5 5.3 %collective-permute-start.1 = (bf16[2,1,48,256]{3,2,1,0:T(8,128)(2,1)S(1)}, bf16[2,1,48,256]{3,2,1,0:T(8,128)(2,1)S(1)}, u32[]{:S(2)}, u32[]{:S(2)}) collective-permute-start(bf16[2,1,48,256]{3,2,1,0:T(8,128)(2,1)S(1)} %get-tuple-element.159), channel_id=1, source_target_pairs={{8,0},{16,8},{24,16},{32,24},{40,32},{48,40},{56,48},{64,56},{72,6... | collective-permute-start | bytes 147464 | tf_op jit(solution)/shard_map/ppermute | solution.py:26
  177.8 1.9 collective-permute-start
  179.8 5.5 %collective-permute-done = bf16[2,1,48,256]{3,2,1,0:T(8,128)(2,1)S(1)} collective-permute-done((bf16[2,1,48,256]{3,2,1,0:T(8,128)(2,1)S(1)}, bf16[2,1,48,256]{3,2,1,0:T(8,128)(2,1)S(1)}, u32[]{:S(2)}, u32[]{:S(2)}) %collective-permute-start) | collective-permute-done | bytes 49184 | tf_op jit(solution)/shard_map/ppermute | solution.py:25
  185.3 4.1 %collective-permute-start.3 = (bf16[2,6,1,256]{3,2,1,0:T(2,128)(2,1)S(1)}, bf16[2,6,1,256]{3,2,1,0:T(2,128)(2,1)S(1)}, u32[]{:S(2)}, u32[]{:S(2)}) collective-permute-start(bf16[2,6,1,256]{3,2,1,0:T(2,128)(2,1)S(1)} %get-tuple-element.157), channel_id=1, source_target_pairs={{1,0},{2,1},{3,2},{4,3},{5,4},{6,5},{7,6},{9,8},{10,9},{11,10},{12... | collective-permute-start | bytes 18440 | tf_op jit(solution)/shard_map/ppermute | solution.py:26
  189.5 1.9 collective-permute-start.2
  191.5 2.3 collective-permute-start.7
  193.7 7.2 %collective-permute-start.6 = (f32[2,6,1]{2,1,0:T(8,128)S(1)}, f32[2,6,1]{2,1,0:T(8,128)S(1)}, u32[]{:S(2)}, u32[]{:S(2)}) collective-permute-start(f32[2,6,1]{2,1,0:T(8,128)S(1)} %get-tuple-element.160), channel_id=1, source_target_pairs={{1,0},{2,1},{3,2},{4,3},{5,4},{6,5},{7,6},{9,8},{10,9},{11,10},{12... | collective-permute-start | bytes 152 | tf_op jit(solution)/shard_map/ppermute | solution.py:26
  200.9 0.1 pad_maximum_fusion
  201.1 0.1 fusion.21
  201.3 0.1 fusion.19
  201.5 0.8 fusion.51
  202.3 0.1 convert_bitcast_fusion
  202.4 1.9 collective-permute-start.9
  204.4 2.4 %collective-permute-start.8 = (bf16[3,1,48,256]{3,2,1,0:T(8,128)(2,1)S(1)}, bf16[3,1,48,256]{3,2,1,0:T(8,128)(2,1)S(1)}, u32[]{:S(2)}, u32[]{:S(2)}) collective-permute-start(bf16[3,1,48,256]{3,2,1,0:T(8,128)(2,1)S(1)} %get-tuple-element.154), channel_id=1, source_target_pairs={{0,8},{8,16},{16,24},{24,32},{32,40},{40,48},{48,56},{56,64},{64,7... | collective-permute-start | bytes 221192 | tf_op jit(solution)/shard_map/ppermute | solution.py:25
  206.9 0.1 multiply_select_fusion.1
  207.0 5.2 %collective-permute-done.8 = bf16[3,1,48,256]{3,2,1,0:T(8,128)(2,1)S(1)} collective-permute-done((bf16[3,1,48,256]{3,2,1,0:T(8,128)(2,1)S(1)}, bf16[3,1,48,256]{3,2,1,0:T(8,128)(2,1)S(1)}, u32[]{:S(2)}, u32[]{:S(2)}) %collective-permute-start.8) | collective-permute-done | bytes 73760 | tf_op jit(solution)/shard_map/ppermute | solution.py:25
  212.2 3.9 %collective-permute-start.11 = (bf16[3,6,1,256]{3,2,1,0:T(2,128)(2,1)S(1)}, bf16[3,6,1,256]{3,2,1,0:T(2,128)(2,1)S(1)}, u32[]{:S(2)}, u32[]{:S(2)}) collective-permute-start(bf16[3,6,1,256]{3,2,1,0:T(2,128)(2,1)S(1)} %get-tuple-element.148), channel_id=1, source_target_pairs={{1,0},{2,1},{3,2},{4,3},{5,4},{6,5},{7,6},{9,8},{10,9},{11,10},{12... | collective-permute-start | bytes 27656 | tf_op jit(solution)/shard_map/ppermute | solution.py:26
  216.1 1.9 collective-permute-start.10
  218.1 0.7 slice_subtract_fusion.2
  218.7 6.7 %collective-permute-done.10 = bf16[3,6,1,256]{3,2,1,0:T(2,128)(2,1)S(1)} collective-permute-done((bf16[3,6,1,256]{3,2,1,0:T(2,128)(2,1)S(1)}, bf16[3,6,1,256]{3,2,1,0:T(2,128)(2,1)S(1)}, u32[]{:S(2)}, u32[]{:S(2)}) %collective-permute-start.10) | collective-permute-done | bytes 9248 | tf_op jit(solution)/shard_map/ppermute | solution.py:25
  225.4 0.1 maximum_convert_fusion
  225.6 1.0 fusion.24
  (71 shorter events, 1.6 us)
Async XLA Ops:
  7.2 70.9 %all-gather.2.cloned.1.call-start = ((), (), s32[]{:S(2)}) async-start(), calls=%async_computation.2 | async-start | bytes 3932160 | tf_op jit(solution)/shard_map/all_gather | solution.py:136
  37.4 17.6 %all-to-all-start = ((bf16[8,192,256]{2,1,0:T(8,128)(2,1)}), bf16[8,192,256]{2,1,0:T(8,128)(2,1)S(1)}, u32[]{:S(2)}, u32[]{:S(2)}) async-start(bf16[8,192,256]{2,1,0:T(8,128)(2,1)} %stack.45), calls=%async_computation | async-start | bytes 1572864 | tf_op jit(solution)/shard_map/all_to_all | solution.py:117
  85.7 8.5 %copy-start = (f32[2048,1536]{1,0:T(8,128)S(1)}, f32[2048,1536]{1,0:T(8,128)}, u32[]{:S(2)}) copy-start(f32[2048,1536]{1,0:T(8,128)} %get-tuple-element.242) | copy-start | bytes 37748740 | tf_op jit(solution)/shard_map/while
  105.8 8.5 %copy-start = (f32[2048,1536]{1,0:T(8,128)S(1)}, f32[2048,1536]{1,0:T(8,128)}, u32[]{:S(2)}) copy-start(f32[2048,1536]{1,0:T(8,128)} %get-tuple-element.242) | copy-start | bytes 37748740 | tf_op jit(solution)/shard_map/while
  125.9 8.5 %copy-start = (f32[2048,1536]{1,0:T(8,128)S(1)}, f32[2048,1536]{1,0:T(8,128)}, u32[]{:S(2)}) copy-start(f32[2048,1536]{1,0:T(8,128)} %get-tuple-element.242) | copy-start | bytes 37748740 | tf_op jit(solution)/shard_map/while
  140.1 31.8 %copy-start.1 = (bf16[4,48,256]{2,1,0:T(8,128)(2,1)S(1)}, bf16[4,48,256]{2,1,0:T(8,128)(2,1)}, u32[]{:S(2)}) copy-start(bf16[4,48,256]{2,1,0:T(8,128)(2,1)} %param.4) | copy-start | bytes 294916
  140.1 26.7 %all-to-all-start.1 = ((f32[8,196,256]{2,1,0:T(8,128)}), f32[8,196,256]{2,1,0:T(8,128)S(1)}, u32[]{:S(2)}, u32[]{:S(2)}) async-start(f32[8,196,256]{2,1,0:T(8,128)} %select_maximum_fusion.1), calls=%async_computation.1 | async-start | bytes 3276800 | tf_op jit(solution)/shard_map/all_to_all | solution.py:166
  167.2 12.5 %collective-permute-start.4 = (f32[2,1,48]{2,1,0:T(1,128)S(1)}, f32[2,1,48]{2,1,0:T(1,128)S(1)}, u32[]{:S(2)}, u32[]{:S(2)}) collective-permute-start(f32[2,1,48]{2,1,0:T(1,128)S(1)} %get-tuple-element.163), channel_id=1, source_target_pairs={{8,0},{16,8},{24,16},{32,24},{40,32},{48,40},{56,48},{64,56},{72,6... | collective-permute-start | bytes 1160 | tf_op jit(solution)/shard_map/ppermute | solution.py:26
  169.1 10.6 %collective-permute-start.5 = (f32[2,1,48]{2,1,0:T(1,128)S(1)}, f32[2,1,48]{2,1,0:T(1,128)S(1)}, u32[]{:S(2)}, u32[]{:S(2)}) collective-permute-start(f32[2,1,48]{2,1,0:T(1,128)S(1)} %get-tuple-element.162), channel_id=1, source_target_pairs={{0,8},{8,16},{16,24},{24,32},{32,40},{40,48},{48,56},{56,64},{64,7... | collective-permute-start | bytes 1160 | tf_op jit(solution)/shard_map/ppermute | solution.py:25
  172.5 7.2 %collective-permute-start.1 = (bf16[2,1,48,256]{3,2,1,0:T(8,128)(2,1)S(1)}, bf16[2,1,48,256]{3,2,1,0:T(8,128)(2,1)S(1)}, u32[]{:S(2)}, u32[]{:S(2)}) collective-permute-start(bf16[2,1,48,256]{3,2,1,0:T(8,128)(2,1)S(1)} %get-tuple-element.159), channel_id=1, source_target_pairs={{8,0},{16,8},{24,16},{32,24},{40,32},{48,40},{56,48},{64,56},{72,6... | collective-permute-start | bytes 147464 | tf_op jit(solution)/shard_map/ppermute | solution.py:26
  177.8 7.5 %collective-permute-start = (bf16[2,1,48,256]{3,2,1,0:T(8,128)(2,1)S(1)}, bf16[2,1,48,256]{3,2,1,0:T(8,128)(2,1)S(1)}, u32[]{:S(2)}, u32[]{:S(2)}) collective-permute-start(bf16[2,1,48,256]{3,2,1,0:T(8,128)(2,1)S(1)} %get-tuple-element.158), channel_id=1, source_target_pairs={{0,8},{8,16},{16,24},{24,32},{32,40},{40,48},{48,56},{56,64},{64,7... | collective-permute-start | bytes 147464 | tf_op jit(solution)/shard_map/ppermute | solution.py:25
  185.3 15.6 %collective-permute-start.3 = (bf16[2,6,1,256]{3,2,1,0:T(2,128)(2,1)S(1)}, bf16[2,6,1,256]{3,2,1,0:T(2,128)(2,1)S(1)}, u32[]{:S(2)}, u32[]{:S(2)}) collective-permute-start(bf16[2,6,1,256]{3,2,1,0:T(2,128)(2,1)S(1)} %get-tuple-element.157), channel_id=1, source_target_pairs={{1,0},{2,1},{3,2},{4,3},{5,4},{6,5},{7,6},{9,8},{10,9},{11,10},{12... | collective-permute-start | bytes 18440 | tf_op jit(solution)/shard_map/ppermute | solution.py:26
  189.5 11.5 %collective-permute-start.2 = (bf16[2,6,1,256]{3,2,1,0:T(2,128)(2,1)S(1)}, bf16[2,6,1,256]{3,2,1,0:T(2,128)(2,1)S(1)}, u32[]{:S(2)}, u32[]{:S(2)}) collective-permute-start(bf16[2,6,1,256]{3,2,1,0:T(2,128)(2,1)S(1)} %get-tuple-element.156), channel_id=1, source_target_pairs={{0,1},{1,2},{2,3},{3,4},{4,5},{5,6},{6,7},{8,9},{9,10},{10,11},{11... | collective-permute-start | bytes 18440 | tf_op jit(solution)/shard_map/ppermute | solution.py:25
  191.5 15.4 %collective-permute-start.7 = (f32[2,6,1]{2,1,0:T(8,128)S(1)}, f32[2,6,1]{2,1,0:T(8,128)S(1)}, u32[]{:S(2)}, u32[]{:S(2)}) collective-permute-start(f32[2,6,1]{2,1,0:T(8,128)S(1)} %get-tuple-element.161), channel_id=1, source_target_pairs={{0,1},{1,2},{2,3},{3,4},{4,5},{5,6},{6,7},{8,9},{9,10},{10,11},{11... | collective-permute-start | bytes 152 | tf_op jit(solution)/shard_map/ppermute | solution.py:25
  193.7 13.1 %collective-permute-start.6 = (f32[2,6,1]{2,1,0:T(8,128)S(1)}, f32[2,6,1]{2,1,0:T(8,128)S(1)}, u32[]{:S(2)}, u32[]{:S(2)}) collective-permute-start(f32[2,6,1]{2,1,0:T(8,128)S(1)} %get-tuple-element.160), channel_id=1, source_target_pairs={{1,0},{2,1},{3,2},{4,3},{5,4},{6,5},{7,6},{9,8},{10,9},{11,10},{12... | collective-permute-start | bytes 152 | tf_op jit(solution)/shard_map/ppermute | solution.py:26
  202.4 4.5 %collective-permute-start.9 = (bf16[3,1,48,256]{3,2,1,0:T(8,128)(2,1)S(1)}, bf16[3,1,48,256]{3,2,1,0:T(8,128)(2,1)S(1)}, u32[]{:S(2)}, u32[]{:S(2)}) collective-permute-start(bf16[3,1,48,256]{3,2,1,0:T(8,128)(2,1)S(1)} %get-tuple-element.155), channel_id=1, source_target_pairs={{8,0},{16,8},{24,16},{32,24},{40,32},{48,40},{56,48},{64,56},{72,6... | collective-permute-start | bytes 221192 | tf_op jit(solution)/shard_map/ppermute | solution.py:26
  204.4 7.8 %collective-permute-start.8 = (bf16[3,1,48,256]{3,2,1,0:T(8,128)(2,1)S(1)}, bf16[3,1,48,256]{3,2,1,0:T(8,128)(2,1)S(1)}, u32[]{:S(2)}, u32[]{:S(2)}) collective-permute-start(bf16[3,1,48,256]{3,2,1,0:T(8,128)(2,1)S(1)} %get-tuple-element.154), channel_id=1, source_target_pairs={{0,8},{8,16},{16,24},{24,32},{32,40},{40,48},{48,56},{56,64},{64,7... | collective-permute-start | bytes 221192 | tf_op jit(solution)/shard_map/ppermute | solution.py:25
  212.2 6.5 %collective-permute-start.11 = (bf16[3,6,1,256]{3,2,1,0:T(2,128)(2,1)S(1)}, bf16[3,6,1,256]{3,2,1,0:T(2,128)(2,1)S(1)}, u32[]{:S(2)}, u32[]{:S(2)}) collective-permute-start(bf16[3,6,1,256]{3,2,1,0:T(2,128)(2,1)S(1)} %get-tuple-element.148), channel_id=1, source_target_pairs={{1,0},{2,1},{3,2},{4,3},{5,4},{6,5},{7,6},{9,8},{10,9},{11,10},{12... | collective-permute-start | bytes 27656 | tf_op jit(solution)/shard_map/ppermute | solution.py:26
  216.1 9.3 %collective-permute-start.10 = (bf16[3,6,1,256]{3,2,1,0:T(2,128)(2,1)S(1)}, bf16[3,6,1,256]{3,2,1,0:T(2,128)(2,1)S(1)}, u32[]{:S(2)}, u32[]{:S(2)}) collective-permute-start(bf16[3,6,1,256]{3,2,1,0:T(2,128)(2,1)S(1)} %get-tuple-element.147), channel_id=1, source_target_pairs={{0,1},{1,2},{2,3},{3,4},{4,5},{5,6},{6,7},{8,9},{9,10},{10,11},{11... | collective-permute-start | bytes 27656 | tf_op jit(solution)/shard_map/ppermute | solution.py:25
Sparse Core Ops, SparseCore 0:
  35.6 42.4 all-gather.1
